TPU v7x, 256 devices: a whole 4x4x8 slice. The times are simulated.
256 devices in a mesh: space: 64 (over z, x, core), head: 4 (over y).
Axes of the slice: x: 4, y: 4, z: 8, core: 2. Of those that a mesh axis runs over, the one named last changes fastest.
Arguments:
- features: bfloat16 [512, 16, 16, 128], P('space', None, None, 'head'), may hold values from -6 to 6
- mask: int32 [512, 16, 16], P('space'), may hold values from 0 to 1, as said below
- conv1_weight: bfloat16 [27, 128, 128], replicated, may hold values from -0.21875 to 0.21875
- conv2_weight: bfloat16 [27, 128, 128], replicated, may hold values from -0.21875 to 0.21875
- down_weight: bfloat16 [8, 128, 512], replicated, may hold values from -0.1875 to 0.1875
- norm_gain: float32 [512], replicated, may hold values from 0.1 to 1.9
- qkv_weight: bfloat16 [512, 3, 512], P(None, None, 'head'), may hold values from -2 to 2
- out_weight: bfloat16 [512, 512], P('head'), may hold values from -0.25 to 0.25
Outputs:
- refined: bfloat16 [512, 16, 16, 128], P('space', None, None, 'head')
- level_out: bfloat16 [16384, 512], P('space', 'head')
Inputs may be any that keep to these rules, and one draw needn't show every extreme that they name: `mask`: A voxel is occupied only inside an active brick of 8^3 aligned voxels; the first brick and its first voxel are always occupied.
All inputs are finite; a program needn't handle non-finite values.
Results may differ from a plain program's by a relative error of at most 0.012.
Values may be sent and summed in bfloat16 or wider, within the bound.
No kernel may reach another device: no remote copies, remote signals or barrier semaphores. Data moves between devices by JAX's collectives and lax.ppermute only.
A program may use at most 64 MiB of HBM per device.

v0:
```python
import jax
import jax.numpy as jnp
from jax import lax
from jax.sharding import PartitionSpec as P

HEADS = 8
KEY_BLOCK = 1024


def with_halo(cells, axis, width):
    count = lax.axis_size(axis)
    ends = count - 1
    head = lax.slice_in_dim(cells, 0, width, axis=0)
    tail = lax.slice_in_dim(cells, cells.shape[0] - width, cells.shape[0], axis=0)
    return jnp.concatenate(
        [
            lax.ppermute(tail, axis, [(i, i + 1) for i in range(ends)]),
            cells,
            lax.ppermute(head, axis, [(i + 1, i) for i in range(ends)]),
        ],
        axis=0,
    )


def convolve(rimmed, weight):
    chans = weight.shape[1]
    kernel = weight.reshape(3, 3, 3, chans, weight.shape[2])
    out = lax.conv_general_dilated(
        rimmed[None],
        kernel,
        window_strides=(1, 1, 1),
        padding=((0, 0), (1, 1), (1, 1)),
        dimension_numbers=("NDHWC", "DHWIO", "NDHWC"),
        preferred_element_type=jnp.float32,
    )
    return out[0]


def to_cells(field):
    nx, ny, nz, count = field.shape
    blocks = field.reshape(nx // 2, 2, ny // 2, 2, nz // 2, 2, count).transpose(0, 2, 4, 1, 3, 5, 6)
    return blocks.reshape(nx // 2 * (ny // 2) * (nz // 2), 8 * count)


def body(
    features, mask, conv1_weight, conv2_weight, down_weight, norm_gain, qkv_weight, out_weight
):
    member = lax.axis_index("head")
    nx, ny, nz, local = features.shape
    width = down_weight.shape[2]
    chans = conv1_weight.shape[1]
    tokens = nx // 2 * (ny // 2) * (nz // 2)
    occupied = mask.astype(jnp.float32)[..., None]
    masked = features * mask.astype(jnp.bfloat16)[..., None]
    rimmed = lax.all_gather(with_halo(masked, "space", 1), "head", axis=3, tiled=True)
    whole_masked = lax.slice_in_dim(rimmed, 1, nx + 1, axis=0)
    pre1 = convolve(rimmed, conv1_weight)
    hidden = (occupied * jax.nn.silu(pre1)).astype(jnp.bfloat16)
    pre2 = convolve(with_halo(hidden, "space", 1), conv2_weight)
    refined_all = (occupied * (whole_masked.astype(jnp.float32) + pre2)).astype(jnp.bfloat16)
    refined = lax.dynamic_slice_in_dim(refined_all, member * local, local, 3)
    coarse = jnp.dot(
        to_cells(refined_all),
        down_weight.reshape(8 * chans, width),
        preferred_element_type=jnp.float32,
    ).astype(jnp.bfloat16)
    wide = coarse.astype(jnp.float32)
    normed = (
        wide * lax.rsqrt(jnp.mean(wide * wide, axis=1, keepdims=True) + 1e-05) * norm_gain
    ).astype(jnp.bfloat16)
    local_cols = qkv_weight.shape[2]
    proj = jnp.dot(
        normed, qkv_weight.reshape(width, 3 * local_cols), preferred_element_type=jnp.float32
    )
    proj = proj.astype(jnp.bfloat16).reshape(tokens, 3, local_cols)
    head_size = width // HEADS
    heads_here = local_cols // head_size
    query = proj[:, 0].reshape(tokens, heads_here, head_size)
    live_cell = (
        mask.reshape(nx // 2, 2, ny // 2, 2, nz // 2, 2)
        .max(axis=(1, 3, 5))
        .reshape(1, -1)
        .astype(jnp.bfloat16)
    )
    span = 2 * local_cols
    live_len = -(-tokens // span) * span
    live_rows = jnp.pad(live_cell, ((0, 0), (0, live_len - tokens))).reshape(-1, span)
    live_count = live_rows.shape[0]
    live_rows = jnp.pad(live_rows, ((0, -(-live_count // 8) * 8 - live_count), (0, 0)))
    piece = jnp.concatenate([proj[:, 1], proj[:, 2]], axis=1)
    piece = jnp.concatenate([piece, live_rows], axis=0)
    rows = piece.shape[0]
    gathered = lax.all_gather(piece[None], "space", axis=0, tiled=True)
    parts = gathered.shape[0]
    count = parts * tokens
    piece_keys = gathered[:, :tokens, :local_cols].reshape(count, heads_here, head_size)
    piece_values = gathered[:, :tokens, local_cols:].reshape(count, heads_here, head_size)
    piece_live = (
        gathered[:, tokens : tokens + live_count].reshape(parts, -1)[:, :tokens].reshape(count)
    )
    bias = jnp.where(piece_live > 0, 0.0, -1e30).astype(jnp.float32)
    scale = head_size ** (-0.5)

    def one_block(carry, block):
        top_old, sums, accum = carry
        block_keys, block_values, block_bias = block
        scores = (
            jnp.einsum("qhd,khd->hqk", query, block_keys, preferred_element_type=jnp.float32)
            * scale
            + block_bias[None, None, :]
        )
        top_new = jnp.maximum(top_old, jnp.max(scores, axis=-1))
        expo = jnp.exp(scores - top_new[..., None])
        factor = jnp.exp(top_old - top_new)
        sums = sums * factor + jnp.sum(expo, axis=-1)
        accum = accum * factor[..., None] + jnp.einsum(
            "hqk,khd->hqd",
            expo.astype(jnp.bfloat16),
            block_values,
            preferred_element_type=jnp.float32,
        )
        return ((top_new, sums, accum), None)

    start_state = (
        jnp.full((heads_here, tokens), -1e30, jnp.float32),
        jnp.zeros((heads_here, tokens), jnp.float32),
        jnp.zeros((heads_here, tokens, head_size), jnp.float32),
    )
    size = KEY_BLOCK if count % KEY_BLOCK == 0 else tokens
    blocks = count // size
    stacked = (
        piece_keys.reshape(blocks, size, heads_here, head_size),
        piece_values.reshape(blocks, size, heads_here, head_size),
        bias.reshape(blocks, size),
    )
    carry, unused = lax.scan(one_block, start_state, stacked)
    top_final, sums, accum = carry
    attn = (
        (accum / sums[..., None])
        .transpose(1, 0, 2)
        .reshape(tokens, local_cols)
        .astype(jnp.bfloat16)
    )
    cols_w = lax.all_to_all(out_weight, "head", 1, 0, tiled=True)
    attn_all = lax.all_gather(attn, "head", axis=1, tiled=True)
    mixed = jnp.dot(attn_all, cols_w, preferred_element_type=jnp.float32)
    mine = lax.dynamic_slice_in_dim(wide, member * local_cols, local_cols, 1)
    level_out = (mine + mixed).astype(jnp.bfloat16)
    return (refined, level_out)


def solution(mesh):
    in_specs = (
        P("space", None, None, "head"),
        P("space", None, None),
        P(),
        P(),
        P(),
        P(),
        P(None, None, "head"),
        P("head", None),
    )
    out_specs = (P("space", None, None, "head"), P("space", "head"))
    return jax.shard_map(body, mesh=mesh, in_specs=in_specs, out_specs=out_specs, check_vma=False)
```

profile of v0, /device:TPU:8, one launch (start us, length us, event | category | flops | bytes accessed | tf_op | source)
XLA Modules:
  0.0 343.7 jit_solution(4440227885603397588)
XLA Ops:
  7.2 1.0 fusion.60
  8.2 2.7 copy.59
  11.1 1.7 collective-permute-start
  12.8 1.3 collective-permute-start.1
  14.2 3.1 collective-permute-done.1
  17.6 45.3 %all_gather.9 = bf16[10,16,16,128]{2,1,0,3:T(8,128)(2,1)} all-gather(bf16[10,16,16,32]{2,1,0,3:T(8,128)(2,1)S(1)} %pad_maximum_fusion), channel_id=1, replica_groups=mesh['space'=64,'head'=4] {'head'}, dimensions={3}, use_global_device_ids=true | all-gather | bytes 819200 | tf_op jit(solution)/shard_map/all_gather | solution.py:55
  62.9 5.2 %copy.60 = bf16[10,16,16,128]{3,1,2,0:T(8,128)(2,1)S(1)} copy(bf16[10,16,16,128]{2,1,0,3:T(8,128)(2,1)} %all_gather.9) | data formatting | bytes 1310720 | tf_op jit(solution)/shard_map/all_gather | solution.py:55
  68.8 0.5 copy-done.5
  69.3 6.2 %fusion.35 = f32[8,16,8,3,128]{4,2,3,1,0:T(8,128)S(1)} fusion(bf16[3,3,3,128,128]{4,3,2,1,0:T(8,128)(2,1)S(1)} %bitcast.110, bf16[10,16,1,7,2,128]{5,3,4,1,0,2:T(8,128)(2,1)S(1)} %slice.51, bf16[10,16,1,8,3,128]{5,3,4,1,0,2:T(8,128)(2,1)S(1)} %copy.63, pred[8,3]{0,1:T(4,128)(4,1)S(1)} %copy-done.7), kind=kOutput, calls=%fused_computation.40 | convolution fusion | flops 2609971200 | bytes 4014104 | tf_op jit(solution)/shard_map/conv_general_dilated | solution.py:28
  76.1 4.3 %collective-permute-start.2 = (bf16[1,16,16,128]{3,1,2,0:T(8,128)(2,1)S(1)}, bf16[1,16,16,128]{3,1,2,0:T(8,128)(2,1)S(1)}, u32[]{:S(2)}, u32[]{:S(2)}) collective-permute-start(bf16[1,16,16,128]{3,1,2,0:T(8,128)(2,1)S(1)} %get-tuple-element.128), channel_id=1, source_target_pairs={{0,4},{4,8},{8,12},{12,16},{16,20},{20,24},{24,28},{28,32},{32,36}... | collective-permute-start | bytes 196616 | tf_op jit(solution)/shard_map/ppermute | solution.py:17
  80.5 1.5 collective-permute-start.3
  82.1 1.2 copy.69
  83.3 0.6 reduce_max.18
  84.1 1.9 collective-permute-done.3
  86.7 0.5 copy-done.6
  87.2 6.2 %fusion.32 = f32[8,16,8,3,128]{4,2,3,1,0:T(8,128)S(1)} fusion(bf16[3,3,3,128,128]{4,3,2,1,0:T(8,128)(2,1)S(1)} %bitcast.111, bf16[10,16,1,7,2,128]{5,3,4,1,0,2:T(8,128)(2,1)S(1)} %slice.55, bf16[10,16,1,8,3,128]{5,3,4,1,0,2:T(8,128)(2,1)S(1)} %copy.66, pred[8,3]{0,1:T(4,128)(4,1)S(1)} %copy-done.7), kind=kOutput, calls=%fused_computation.39 | convolution fusion | flops 2609971200 | bytes 4014104 | tf_op jit(solution)/shard_map/conv_general_dilated | solution.py:28
  94.4 0.5 multiply_reduce_fusion
  95.5 0.8 copy.74
  96.3 0.8 copy.79
  97.1 4.5 %all-to-all-start = ((bf16[128,4,128]{0,2,1:T(8,128)(2,1)}), bf16[128,4,128]{0,2,1:T(8,128)(2,1)S(1)}, u32[]{:S(2)}, u32[]{:S(2)}) async-start(bf16[128,4,128]{0,2,1:T(8,128)(2,1)} %bitcast.24), calls=%async_computation | async-start | bytes 262144 | tf_op jit(solution)/shard_map/all_to_all | solution.py:144
  101.8 0.9 copy.81
  102.7 3.4 all-to-all-done
  106.2 82.1 %all-gather.3.cloned.1.call-done = bf16[16896,256]{1,0:T(8,128)(2,1)} async-done(((bf16[264,256]{1,0:T(8,128)(2,1)}), bf16[16896,256]{1,0:T(8,128)(2,1)}) %all-gather.3.cloned.1.call-update) | async-done | bytes 8650768 | tf_op jit(solution)/shard_map/all_gather | solution.py:93
  188.3 1.1 fusion.49
  189.5 6.0 %fusion.56 = (bf16[64,256,128]{2,1,0:T(8,128)(2,1)}, bf16[64,256,128]{2,1,0:T(8,128)(2,1)}) fusion(bf16[64,264,256]{2,1,0:T(8,128)(2,1)} %bitcast.93), kind=kLoop, calls=%fused_computation.77 | loop fusion | bytes 16777216 | tf_op jit(solution)/shard_map/slice | solution.py:97
  195.5 14.7 %reshape.108 = bf16[16,1024,2,64]{3,2,1,0:T(2,128)(2,1)} reshape(bf16[64,256,128]{2,1,0:T(8,128)(2,1)} %get-tuple-element.124) | data formatting | bytes 8388608 | tf_op jit(solution)/shard_map/reshape;reshape | solution.py:133
  210.2 20.1 %copy.78 = bf16[16,1024,2,64]{1,3,2,0:T(8,128)(2,1)} copy(bf16[16,1024,2,64]{3,2,1,0:T(2,128)(2,1)} %reshape.108) | data formatting | bytes 8388608
  230.3 14.7 %reshape.107 = bf16[16,1024,2,64]{3,2,1,0:T(2,128)(2,1)} reshape(bf16[64,256,128]{2,1,0:T(8,128)(2,1)} %get-tuple-element.125) | data formatting | bytes 8388608 | tf_op jit(solution)/shard_map/reshape;reshape | solution.py:132
  245.0 20.1 %copy.77 = bf16[16,1024,2,64]{1,3,2,0:T(8,128)(2,1)} copy(bf16[16,1024,2,64]{3,2,1,0:T(2,128)(2,1)} %reshape.107) | data formatting | bytes 8388608
  265.1 58.0 %while.15 = (s32[]{:T(128)}, f32[2,256]{1,0:T(2,128)S(1)}, f32[2,256]{1,0:T(2,128)S(1)}, f32[2,256,64]{1,2,0:T(8,128)S(1)}, bf16[16,1024,2,64]{1,3,2,0:T(8,128)(...) while((s32[]{:T(128)}, f32[2,256]{1,0:T(2,128)S(1)}, ...), condition=%wide.region_5.6_spmd.clone, body=%wide.region_2.5_spmd.clone.sunk | while | flops 140085760 | bytes 7196805 | solution.py:136
  265.1 1.5 bitcast_reduce_fusion.2
  267.1 1.6 convolution_add_fusion.3
  268.7 1.5 bitcast_reduce_fusion.2
  270.7 1.6 convolution_add_fusion.3
  272.4 1.5 bitcast_reduce_fusion.2
  274.4 1.6 convolution_add_fusion.3
  276.0 1.5 bitcast_reduce_fusion.2
  278.0 1.6 convolution_add_fusion.3
  279.6 1.5 bitcast_reduce_fusion.2
  281.6 1.6 convolution_add_fusion.3
  283.3 1.5 bitcast_reduce_fusion.2
  285.3 1.6 convolution_add_fusion.3
  286.9 1.5 bitcast_reduce_fusion.2
  288.9 1.6 convolution_add_fusion.3
  290.5 1.5 bitcast_reduce_fusion.2
  292.5 1.6 convolution_add_fusion.3
  294.1 1.5 bitcast_reduce_fusion.2
  296.1 1.6 convolution_add_fusion.3
  297.8 1.5 bitcast_reduce_fusion.2
  299.8 1.6 convolution_add_fusion.3
  301.4 1.5 bitcast_reduce_fusion.2
  303.4 1.6 convolution_add_fusion.3
  305.0 1.5 bitcast_reduce_fusion.2
  307.0 1.6 convolution_add_fusion.3
  308.7 1.5 bitcast_reduce_fusion.2
  310.7 1.6 convolution_add_fusion.3
  312.3 1.5 bitcast_reduce_fusion.2
  314.3 1.6 convolution_add_fusion.3
  315.9 1.5 bitcast_reduce_fusion.2
  317.9 1.6 convolution_add_fusion.3
  319.5 1.5 bitcast_reduce_fusion.2
  321.6 1.6 convolution_add_fusion.3
  323.2 12.8 %all_gather.11 = bf16[256,512]{0,1:T(8,128)(2,1)S(1)} all-gather(bf16[256,128]{0,1:T(8,128)(2,1)S(1)} %bitcast.109), channel_id=1, replica_groups=mesh['space'=64,'head'=4] {'head'}, dimensions={1}, use_global_device_ids=true | all-gather | bytes 327680 | tf_op jit(solution)/shard_map/all_gather | solution.py:145
  336.0 0.9 fusion.39
  (130 shorter events, 13.2 us)
Async XLA Ops:
  7.2 87.3 %copy-start = (bf16[8,128,512]{2,1,0:T(8,128)(2,1)S(1)}, bf16[8,128,512]{2,1,0:T(8,128)(2,1)}, u32[]{:S(2)}) copy-start(bf16[8,128,512]{2,1,0:T(8,128)(2,1)} %param.14) | copy-start | bytes 3145732
  7.2 181.2 %all-gather.3.cloned.1.call-start = ((), (), s32[]{:S(2)}) async-start(), calls=%async_computation.1 | async-start | bytes 8785920 | tf_op jit(solution)/shard_map/all_gather | solution.py:93
  11.1 3.1 collective-permute-start
  12.8 4.5 %collective-permute-start.1 = (bf16[1,16,16,32]{2,1,0,3:T(8,128)(2,1)S(1)}, bf16[1,16,16,32]{2,1,0,3:T(8,128)(2,1)S(1)}, u32[]{:S(2)}, u32[]{:S(2)}) collective-permute-start(bf16[1,16,16,32]{2,1,0,3:T(8,128)(2,1)S(1)} %get-tuple-element.127), channel_id=1, source_target_pairs={{4,0},{8,4},{12,8},{16,12},{20,16},{24,20},{28,24},{32,28},{36,32}... | collective-permute-start | bytes 49160 | tf_op jit(solution)/shard_map/ppermute | solution.py:19
  68.1 1.2 copy-start.5
  68.1 1.2 copy-start.7
  75.5 6.5 %copy-start.2 = (s32[8,16,16]{2,1,0:T(8,128)S(1)}, s32[8,16,16]{2,1,0:T(8,128)}, u32[]{:S(2)}) copy-start(s32[8,16,16]{2,1,0:T(8,128)} %param.11) | copy-start | bytes 24580
  76.1 7.9 %collective-permute-start.2 = (bf16[1,16,16,128]{3,1,2,0:T(8,128)(2,1)S(1)}, bf16[1,16,16,128]{3,1,2,0:T(8,128)(2,1)S(1)}, u32[]{:S(2)}, u32[]{:S(2)}) collective-permute-start(bf16[1,16,16,128]{3,1,2,0:T(8,128)(2,1)S(1)} %get-tuple-element.128), channel_id=1, source_target_pairs={{0,4},{4,8},{8,12},{12,16},{16,20},{20,24},{24,28},{28,32},{32,36}... | collective-permute-start | bytes 196616 | tf_op jit(solution)/shard_map/ppermute | solution.py:17
  80.5 5.5 %collective-permute-start.3 = (bf16[1,16,16,128]{3,1,2,0:T(8,128)(2,1)S(1)}, bf16[1,16,16,128]{3,1,2,0:T(8,128)(2,1)S(1)}, u32[]{:S(2)}, u32[]{:S(2)}) collective-permute-start(bf16[1,16,16,128]{3,1,2,0:T(8,128)(2,1)S(1)} %get-tuple-element.129), channel_id=1, source_target_pairs={{4,0},{8,4},{12,8},{16,12},{20,16},{24,20},{28,24},{32,28},{36,32}... | collective-permute-start | bytes 196616 | tf_op jit(solution)/shard_map/ppermute | solution.py:19
  86.0 1.2 copy-start.6
  94.1 0.9 copy-start.4
  94.4 1.9 copy-start.3
  97.1 9.0 %all-to-all-start = ((bf16[128,4,128]{0,2,1:T(8,128)(2,1)}), bf16[128,4,128]{0,2,1:T(8,128)(2,1)S(1)}, u32[]{:S(2)}, u32[]{:S(2)}) async-start(bf16[128,4,128]{0,2,1:T(8,128)(2,1)} %bitcast.24), calls=%async_computation | async-start | bytes 262144 | tf_op jit(solution)/shard_map/all_to_all | solution.py:144
  323.1 13.7 %copy-start.1 = (bf16[8,128,512]{2,1,0:T(8,128)(2,1)S(1)}, bf16[8,128,512]{2,1,0:T(8,128)(2,1)}, u32[]{:S(2)}) copy-start(bf16[8,128,512]{2,1,0:T(8,128)(2,1)} %param.14) | copy-start | bytes 3145732
Sparse Core Ops, SparseCore 0:
  96.4 91.8 all-gather.2
where the time goes:
time: 347 us; the launch traced here: 344 us
  local copies, waits for them, and re-layouts  91.5 us (26%)
  waiting for transfers between devices  90.5 us (26%)
  matrix products  62.8 us (18%)
  blocking collectives  58.1 us (17%)
  between operations  14.4 us (4%)
  starting transfers between devices  13.4 us (4%)
  other arithmetic  12.2 us (4%)
    all_gather x1, waiting for transfers between devices, body(): gathered = lax.all_gather(piece[None], 'space', axis=0, tiled=True)  82.1 us
    unnamed x22, local copies, waits for them, and re-layouts  46.9 us
    all_gather x1, blocking collectives, body(): lax.all_gather(with_halo(masked, 'space', 1), 'head', axis=3, tiled=True)  45.3 us
    dot_general x16, matrix products, one_block(): jnp.einsum('hqk,khd->hqd', expo.astype(jnp.bfloat16), block_values, prefe...  25.1 us
    dot_general x16, matrix products, one_block(): jnp.einsum('qhd,khd->hqk', query, block_keys, preferred_element_type=jnp....  23.6 us
    another operation x1, local copies, waits for them, and re-layouts, body(): piece_values.reshape(blocks, size, heads_here, head_size)  14.7 us
    another operation x1, local copies, waits for them, and re-layouts, body(): piece_keys.reshape(blocks, size, heads_here, head_size)  14.7 us
    all_gather x1, blocking collectives, body(): attn_all = lax.all_gather(attn, 'head', axis=1, tiled=True)  12.8 us
  transfers between devices with their start and end apart: 6, of which 4 were waited for; matrix products, arithmetic and copies ran while one was open for 1% of the time, Pallas kernels for 0%

commit v1 on v0

--- a/solution.py
+++ b/solution.py
@@ -141,7 +141,12 @@
         .reshape(tokens, local_cols)
         .astype(jnp.bfloat16)
     )
-    cols_w = lax.all_to_all(out_weight, "head", 1, 0, tiled=True)
+    cols_w = jnp.concatenate(
+        lax.all_to_all(
+            jnp.stack(jnp.split(out_weight, lax.axis_size("head"), axis=1)), "head", 0, 0
+        ),
+        axis=0,
+    )
     attn_all = lax.all_gather(attn, "head", axis=1, tiled=True)
     mixed = jnp.dot(attn_all, cols_w, preferred_element_type=jnp.float32)
     mine = lax.dynamic_slice_in_dim(wide, member * local_cols, local_cols, 1)

time: 347 us -> 347 us (level)
    all_gather x1, waiting for transfers between devices: 82.1 us -> 85.7 us  [body(): gathered = lax.all_gather(piece[None], 'space', axis=0, tiled=True)]
    unnamed x22 -> x21, local copies, waits for them, and re-layouts: 46.9 us -> 46.2 us
  transfers between devices with their start and end apart: 6 -> 6, of which waited for: 4 -> 3; matrix products, arithmetic and copies ran while one was open for 1% -> 40% of each run, Pallas kernels for 0% -> 0%
where the time goes in v1:
time: 347 us; the launch traced here: 344 us
  local copies, waits for them, and re-layouts  90.8 us (26%)
  waiting for transfers between devices  90.7 us (26%)
  matrix products  62.8 us (18%)
  blocking collectives  58.1 us (17%)
  between operations  14.4 us (4%)
  starting transfers between devices  13.4 us (4%)
  other arithmetic  12.8 us (4%)
    all_gather x1, waiting for transfers between devices, body(): gathered = lax.all_gather(piece[None], 'space', axis=0, tiled=True)  85.7 us
    unnamed x21, local copies, waits for them, and re-layouts  46.2 us
    all_gather x1, blocking collectives, body(): lax.all_gather(with_halo(masked, 'space', 1), 'head', axis=3, tiled=True)  45.3 us
    dot_general x16, matrix products, one_block(): jnp.einsum('hqk,khd->hqd', expo.astype(jnp.bfloat16), block_values, prefe...  25.1 us
    dot_general x16, matrix products, one_block(): jnp.einsum('qhd,khd->hqk', query, block_keys, preferred_element_type=jnp....  23.6 us
    another operation x1, local copies, waits for them, and re-layouts, body(): piece_values.reshape(blocks, size, heads_here, head_size)  14.7 us
    another operation x1, local copies, waits for them, and re-layouts, body(): piece_keys.reshape(blocks, size, heads_here, head_size)  14.7 us
    all_gather x1, blocking collectives, body(): attn_all = lax.all_gather(attn, 'head', axis=1, tiled=True)  12.8 us
  transfers between devices with their start and end apart: 6, of which 3 were waited for; matrix products, arithmetic and copies ran while one was open for 40% of the time, Pallas kernels for 0%

profile of v1, /device:TPU:8, one launch (start us, length us, event | category | flops | bytes accessed | tf_op | source)
XLA Modules:
  0.0 343.9 jit_solution(16079363204630740678)
XLA Ops:
  7.2 1.0 fusion.60
  8.2 2.7 copy.57
  11.1 1.7 collective-permute-start
  12.8 1.3 collective-permute-start.1
  14.2 3.1 collective-permute-done.1
  17.6 45.3 %all_gather.9 = bf16[10,16,16,128]{2,1,0,3:T(8,128)(2,1)} all-gather(bf16[10,16,16,32]{2,1,0,3:T(8,128)(2,1)S(1)} %pad_maximum_fusion), channel_id=1, replica_groups=mesh['space'=64,'head'=4] {'head'}, dimensions={3}, use_global_device_ids=true | all-gather | bytes 819200 | tf_op jit(solution)/shard_map/all_gather | solution.py:55
  62.9 5.2 %copy.58 = bf16[10,16,16,128]{3,1,2,0:T(8,128)(2,1)S(1)} copy(bf16[10,16,16,128]{2,1,0,3:T(8,128)(2,1)} %all_gather.9) | data formatting | bytes 1310720 | tf_op jit(solution)/shard_map/all_gather | solution.py:55
  68.8 0.5 copy-done.5
  69.3 6.2 %fusion.35 = f32[8,16,8,3,128]{4,2,3,1,0:T(8,128)S(1)} fusion(bf16[3,3,3,128,128]{4,3,2,1,0:T(8,128)(2,1)S(1)} %bitcast.115, bf16[10,16,1,7,2,128]{5,3,4,1,0,2:T(8,128)(2,1)S(1)} %slice.51, bf16[10,16,1,8,3,128]{5,3,4,1,0,2:T(8,128)(2,1)S(1)} %copy.61, pred[8,3]{0,1:T(4,128)(4,1)S(1)} %copy-done.7), kind=kOutput, calls=%fused_computation.40 | convolution fusion | flops 2609971200 | bytes 4014104 | tf_op jit(solution)/shard_map/conv_general_dilated | solution.py:28
  76.1 4.3 %collective-permute-start.2 = (bf16[1,16,16,128]{3,1,2,0:T(8,128)(2,1)S(1)}, bf16[1,16,16,128]{3,1,2,0:T(8,128)(2,1)S(1)}, u32[]{:S(2)}, u32[]{:S(2)}) collective-permute-start(bf16[1,16,16,128]{3,1,2,0:T(8,128)(2,1)S(1)} %get-tuple-element.128), channel_id=1, source_target_pairs={{0,4},{4,8},{8,12},{12,16},{16,20},{20,24},{24,28},{28,32},{32,36}... | collective-permute-start | bytes 196616 | tf_op jit(solution)/shard_map/ppermute | solution.py:17
  80.5 1.5 collective-permute-start.3
  82.1 1.2 copy.67
  83.3 0.6 reduce_max.18
  84.1 1.9 collective-permute-done.3
  86.7 0.5 copy-done.6
  87.2 6.2 %fusion.32 = f32[8,16,8,3,128]{4,2,3,1,0:T(8,128)S(1)} fusion(bf16[3,3,3,128,128]{4,3,2,1,0:T(8,128)(2,1)S(1)} %bitcast.116, bf16[10,16,1,7,2,128]{5,3,4,1,0,2:T(8,128)(2,1)S(1)} %slice.55, bf16[10,16,1,8,3,128]{5,3,4,1,0,2:T(8,128)(2,1)S(1)} %copy.64, pred[8,3]{0,1:T(4,128)(4,1)S(1)} %copy-done.7), kind=kOutput, calls=%fused_computation.39 | convolution fusion | flops 2609971200 | bytes 4014104 | tf_op jit(solution)/shard_map/conv_general_dilated | solution.py:28
  94.4 0.5 multiply_reduce_fusion
  95.5 0.8 copy.72
  96.4 0.7 pad_maximum_fusion.1
  97.0 4.5 %all-to-all-start = ((bf16[4,128,128]{2,1,0:T(8,128)(2,1)}), bf16[4,128,128]{2,1,0:T(8,128)(2,1)S(1)}, u32[]{:S(2)}, u32[]{:S(2)}) async-start(bf16[4,128,128]{2,1,0:T(8,128)(2,1)} %pad_maximum_fusion.1), calls=%async_computation | async-start | bytes 262144 | tf_op jit(solution)/shard_map/all_to_all | solution.py:145
  101.8 0.9 copy.77
  102.7 85.7 %all-gather.3.cloned.1.call-done = bf16[16896,256]{1,0:T(8,128)(2,1)} async-done(((bf16[264,256]{1,0:T(8,128)(2,1)}), bf16[16896,256]{1,0:T(8,128)(2,1)}) %all-gather.3.cloned.1.call-update) | async-done | bytes 8650768 | tf_op jit(solution)/shard_map/all_gather | solution.py:93
  188.3 1.1 fusion.49
  189.5 6.0 %fusion.56 = (bf16[64,256,128]{2,1,0:T(8,128)(2,1)}, bf16[64,256,128]{2,1,0:T(8,128)(2,1)}) fusion(bf16[64,264,256]{2,1,0:T(8,128)(2,1)} %bitcast.99), kind=kLoop, calls=%fused_computation.82 | loop fusion | bytes 16777216 | tf_op jit(solution)/shard_map/slice | solution.py:97
  195.5 14.7 %reshape.109 = bf16[16,1024,2,64]{3,2,1,0:T(2,128)(2,1)} reshape(bf16[64,256,128]{2,1,0:T(8,128)(2,1)} %get-tuple-element.124) | data formatting | bytes 8388608 | tf_op jit(solution)/shard_map/reshape;reshape | solution.py:133
  210.2 20.1 %copy.76 = bf16[16,1024,2,64]{1,3,2,0:T(8,128)(2,1)} copy(bf16[16,1024,2,64]{3,2,1,0:T(2,128)(2,1)} %reshape.109) | data formatting | bytes 8388608
  230.3 14.7 %reshape.108 = bf16[16,1024,2,64]{3,2,1,0:T(2,128)(2,1)} reshape(bf16[64,256,128]{2,1,0:T(8,128)(2,1)} %get-tuple-element.125) | data formatting | bytes 8388608 | tf_op jit(solution)/shard_map/reshape;reshape | solution.py:132
  245.0 20.2 %copy.75 = bf16[16,1024,2,64]{1,3,2,0:T(8,128)(2,1)} copy(bf16[16,1024,2,64]{3,2,1,0:T(2,128)(2,1)} %reshape.108) | data formatting | bytes 8388608
  265.2 58.0 %while.15 = (s32[]{:T(128)}, f32[2,256]{1,0:T(2,128)S(1)}, f32[2,256]{1,0:T(2,128)S(1)}, f32[2,256,64]{1,2,0:T(8,128)S(1)}, bf16[16,1024,2,64]{1,3,2,0:T(8,128)(...) while((s32[]{:T(128)}, f32[2,256]{1,0:T(2,128)S(1)}, ...), condition=%wide.region_5.6_spmd.clone, body=%wide.region_2.5_spmd.clone.sunk | while | flops 140085760 | bytes 7196805 | solution.py:136
  265.2 1.5 bitcast_reduce_fusion.2
  267.2 1.6 convolution_add_fusion.3
  268.9 1.5 bitcast_reduce_fusion.2
  270.4 0.5 fusion.79
  270.9 1.6 convolution_add_fusion.3
  272.5 1.5 bitcast_reduce_fusion.2
  274.5 1.6 convolution_add_fusion.3
  276.1 1.5 bitcast_reduce_fusion.2
  278.1 1.6 convolution_add_fusion.3
  279.7 1.5 bitcast_reduce_fusion.2
  281.7 1.6 convolution_add_fusion.3
  283.4 1.5 bitcast_reduce_fusion.2
  285.4 1.6 convolution_add_fusion.3
  287.0 1.5 bitcast_reduce_fusion.2
  289.0 1.6 convolution_add_fusion.3
  290.6 1.5 bitcast_reduce_fusion.2
  292.6 1.6 convolution_add_fusion.3
  294.3 1.5 bitcast_reduce_fusion.2
  296.3 1.6 convolution_add_fusion.3
  297.9 1.5 bitcast_reduce_fusion.2
  299.9 1.6 convolution_add_fusion.3
  301.5 1.5 bitcast_reduce_fusion.2
  303.5 1.6 convolution_add_fusion.3
  305.1 1.5 bitcast_reduce_fusion.2
  307.2 1.6 convolution_add_fusion.3
  308.8 1.5 bitcast_reduce_fusion.2
  310.8 1.6 convolution_add_fusion.3
  312.4 1.5 bitcast_reduce_fusion.2
  314.4 1.6 convolution_add_fusion.3
  316.0 1.5 bitcast_reduce_fusion.2
  318.0 1.6 convolution_add_fusion.3
  319.7 1.5 bitcast_reduce_fusion.2
  321.7 1.6 convolution_add_fusion.3
  323.3 12.8 %all_gather.11 = bf16[256,512]{0,1:T(8,128)(2,1)S(1)} all-gather(bf16[256,128]{0,1:T(8,128)(2,1)S(1)} %bitcast.114), channel_id=1, replica_groups=mesh['space'=64,'head'=4] {'head'}, dimensions={1}, use_global_device_ids=true | all-gather | bytes 327680 | tf_op jit(solution)/shard_map/all_gather | solution.py:150
  336.1 0.9 fusion.39
  (130 shorter events, 12.6 us)
Async XLA Ops:
  7.2 87.3 %copy-start = (bf16[8,128,512]{2,1,0:T(8,128)(2,1)S(1)}, bf16[8,128,512]{2,1,0:T(8,128)(2,1)}, u32[]{:S(2)}) copy-start(bf16[8,128,512]{2,1,0:T(8,128)(2,1)} %param.14) | copy-start | bytes 3145732
  7.2 181.2 %all-gather.3.cloned.1.call-start = ((), (), s32[]{:S(2)}) async-start(), calls=%async_computation.1 | async-start | bytes 8785920 | tf_op jit(solution)/shard_map/all_gather | solution.py:93
  11.1 3.1 collective-permute-start
  12.8 4.5 %collective-permute-start.1 = (bf16[1,16,16,32]{2,1,0,3:T(8,128)(2,1)S(1)}, bf16[1,16,16,32]{2,1,0,3:T(8,128)(2,1)S(1)}, u32[]{:S(2)}, u32[]{:S(2)}) collective-permute-start(bf16[1,16,16,32]{2,1,0,3:T(8,128)(2,1)S(1)} %get-tuple-element.127), channel_id=1, source_target_pairs={{4,0},{8,4},{12,8},{16,12},{20,16},{24,20},{28,24},{32,28},{36,32}... | collective-permute-start | bytes 49160 | tf_op jit(solution)/shard_map/ppermute | solution.py:19
  68.1 1.2 copy-start.5
  68.1 1.2 copy-start.7
  75.5 6.5 %copy-start.2 = (s32[8,16,16]{2,1,0:T(8,128)S(1)}, s32[8,16,16]{2,1,0:T(8,128)}, u32[]{:S(2)}) copy-start(s32[8,16,16]{2,1,0:T(8,128)} %param.11) | copy-start | bytes 24580
  76.1 7.9 %collective-permute-start.2 = (bf16[1,16,16,128]{3,1,2,0:T(8,128)(2,1)S(1)}, bf16[1,16,16,128]{3,1,2,0:T(8,128)(2,1)S(1)}, u32[]{:S(2)}, u32[]{:S(2)}) collective-permute-start(bf16[1,16,16,128]{3,1,2,0:T(8,128)(2,1)S(1)} %get-tuple-element.128), channel_id=1, source_target_pairs={{0,4},{4,8},{8,12},{12,16},{16,20},{20,24},{24,28},{28,32},{32,36}... | collective-permute-start | bytes 196616 | tf_op jit(solution)/shard_map/ppermute | solution.py:17
  80.5 5.5 %collective-permute-start.3 = (bf16[1,16,16,128]{3,1,2,0:T(8,128)(2,1)S(1)}, bf16[1,16,16,128]{3,1,2,0:T(8,128)(2,1)S(1)}, u32[]{:S(2)}, u32[]{:S(2)}) collective-permute-start(bf16[1,16,16,128]{3,1,2,0:T(8,128)(2,1)S(1)} %get-tuple-element.129), channel_id=1, source_target_pairs={{4,0},{8,4},{12,8},{16,12},{20,16},{24,20},{28,24},{32,28},{36,32}... | collective-permute-start | bytes 196616 | tf_op jit(solution)/shard_map/ppermute | solution.py:19
  86.0 1.2 copy-start.6
  94.1 0.9 copy-start.4
  94.4 1.9 copy-start.3
  97.0 239.1 %all-to-all-start = ((bf16[4,128,128]{2,1,0:T(8,128)(2,1)}), bf16[4,128,128]{2,1,0:T(8,128)(2,1)S(1)}, u32[]{:S(2)}, u32[]{:S(2)}) async-start(bf16[4,128,128]{2,1,0:T(8,128)(2,1)} %pad_maximum_fusion.1), calls=%async_computation | async-start | bytes 262144 | tf_op jit(solution)/shard_map/all_to_all | solution.py:145
  323.3 13.8 %copy-start.1 = (bf16[8,128,512]{2,1,0:T(8,128)(2,1)S(1)}, bf16[8,128,512]{2,1,0:T(8,128)(2,1)}, u32[]{:S(2)}) copy-start(bf16[8,128,512]{2,1,0:T(8,128)(2,1)} %param.14) | copy-start | bytes 3145732
Sparse Core Ops, SparseCore 0:
  96.5 91.8 all-gather.2
